TPU v7x, 512 devices: a whole 4x8x8 slice. The times are simulated.
512 devices in a mesh: ctx: 16 (over y, x_hi), tp: 32 (over z, x_lo, core).
Axes of the slice: x: 4 (x_hi: 2, x_lo: 2; x = x_hi * 2 + x_lo), y: 8, z: 8, core: 2. Of those that a mesh axis runs over, the one named last changes fastest.
Arguments:
- resid_in: bfloat16 [2048, 4096], P('ctx', 'tp'), may hold values from -6 to 6
- feats: bfloat16 [2048, 3, 4096], P('ctx', None, 'tp'), may hold values from -6 to 6
- short_filter: float32 [3, 3, 4096], P(None, None, 'tp'), may hold values from -3.5 to 3.5
- residues: float32 [4096, 16], P('tp'), may hold values from -4 to 4
- rates: float32 [4096, 16], P('tp'), may hold values from 0.00014648438 to 0.03
- out_weight: bfloat16 [4096, 4096], P('tp'), may hold values from -0.1875 to 0.1875
- norm_gain: float32 [4096], replicated, may hold values from 0.1 to 1.9
- attn_weight: bfloat16 [4096, 3, 4096], P(None, None, 'tp'), may hold values from -1 to 1
Outputs:
- hyena_out: bfloat16 [2048, 4096], P('ctx', 'tp')
- context: bfloat16 [2048, 4096], P('ctx', 'tp')
All inputs are finite; a program needn't handle non-finite values.
Results may differ from a plain program's by a relative error of at most 0.01.
Values may be sent and summed in bfloat16 or wider, within the bound.
No kernel may reach another device: no remote copies, remote signals or barrier semaphores. Data moves between devices by JAX's collectives and lax.ppermute only.
A program may use at most 192 MiB of HBM per device.

v0:
```python
import math
import jax
import jax.numpy as jnp
from jax import lax
from jax.sharding import PartitionSpec as P

HEAD_DIM = 128
eps_norm = 1e-05
rope_base = 10000.0
mask_fill = -1e30
highest = lax.Precision.HIGHEST


def shifted(value, axis, steps):
    count = lax.axis_size(axis)
    initial, last = (max(0, -steps), min(count, count - steps))
    return lax.ppermute(value, axis, [(source, source + steps) for source in range(initial, last)])


def toeplitz_lower(filter_taps):
    chan_count, block_size = filter_taps.shape
    padded = jnp.concatenate(
        [jnp.zeros((chan_count, block_size - 1), jnp.float32), filter_taps], axis=1
    )
    flipped = padded[:, ::-1]
    tiled = jnp.tile(flipped, (1, block_size))
    offset = block_size - 1
    window = tiled[:, offset : offset + block_size * (2 * block_size - 2)]
    return window.reshape(chan_count, block_size, 2 * block_size - 2)[:, :, :block_size]


def modal_conv(signal, residues, rates, start_state):
    chan_count, length = signal.shape
    block_size = math.gcd(length, 128)
    block_count = length // block_size
    weight = residues * jnp.sqrt(1.0 - jnp.exp(-2.0 * rates))
    lag_steps = jnp.arange(block_size, dtype=jnp.float32)
    powers = jnp.exp(-rates[:, :, None] * lag_steps)
    filter_taps = jnp.sum(weight[:, :, None] * powers, axis=1)
    toeplitz = toeplitz_lower(filter_taps)
    blocks = signal.reshape(chan_count, block_count, block_size)
    inner_part = jnp.einsum("cij,cnj->cni", toeplitz, blocks, precision=highest)
    tail_powers = jnp.exp(-rates[:, :, None] * (block_size - lag_steps))
    end_states = jnp.einsum("cnj,cmj->cnm", blocks, tail_powers, precision=highest)
    block_steps = jnp.arange(block_count, dtype=jnp.float32)
    gap_count = block_steps[:, None] - 1.0 - block_steps[None, :]
    live_mask = gap_count >= 0.0
    carry_mat = jnp.where(
        live_mask, jnp.exp(-rates[:, :, None, None] * block_size * jnp.maximum(gap_count, 0.0)), 0.0
    )
    states = jnp.einsum("cmnk,ckm->cnm", carry_mat, end_states, precision=highest)
    states = (
        states
        + jnp.exp(-rates[:, None, :] * block_size * block_steps[None, :, None])
        * start_state[:, None, :]
    )
    cross_part = jnp.einsum("cnm,cmi->cni", states * weight[:, None, :], powers, precision=highest)
    return (inner_part + cross_part).reshape(chan_count, length)


def short_mix(feats, short_filter):
    row_count = feats.shape[0]
    prior_feats = shifted(feats[-2:], "ctx", 1)
    joined = jnp.concatenate([prior_feats, feats], axis=0).astype(jnp.float32)
    return (
        short_filter[0] * joined[2:]
        + short_filter[1] * joined[1 : row_count + 1]
        + short_filter[2] * joined[:row_count]
    )


def rotary_turn(vectors, positions):
    half_dim = vectors.shape[-1] // 2
    frequency = rope_base ** (-jnp.arange(half_dim, dtype=jnp.float32) * 2.0 / vectors.shape[-1])
    angles = positions.astype(jnp.float32)[:, None] * frequency[None, :]
    cosine = jnp.cos(angles)[:, None, :]
    sine_part = jnp.sin(angles)[:, None, :]
    first_half = vectors[..., :half_dim]
    second = vectors[..., half_dim:]
    return jnp.concatenate(
        [first_half * cosine - second * sine_part, second * cosine + first_half * sine_part],
        axis=-1,
    )


def attend_tile(running, query_rows, query_pos, key_block, value_block, key_start):
    run_peak, denom, accumulated = running
    block_size = key_block.shape[0]
    score_scale = 1.0 / math.sqrt(key_block.shape[2])
    key_pos = key_start + jnp.arange(block_size, dtype=jnp.int32)
    scores = (
        jnp.einsum("shd,khd->hsk", query_rows, key_block, preferred_element_type=jnp.float32)
        * score_scale
    )
    allowed = (query_pos[:, None] >= key_pos[None, :])[None]
    masked = jnp.where(allowed, scores, mask_fill)
    new_peak = jnp.maximum(run_peak, jnp.max(masked, axis=2))
    weights = jnp.where(allowed, jnp.exp(masked - new_peak[:, :, None]), 0.0)
    factor = jnp.exp(run_peak - new_peak)
    denom = denom * factor + jnp.sum(weights, axis=2)
    accumulated = accumulated * factor[:, :, None] + jnp.einsum(
        "hsk,khd->hsd",
        weights.astype(jnp.bfloat16),
        value_block,
        preferred_element_type=jnp.float32,
    )
    return (new_peak, denom, accumulated)


def empty_state(head_count, rows):
    return (
        jnp.full((head_count, rows), mask_fill, jnp.float32),
        jnp.zeros((head_count, rows), jnp.float32),
        jnp.zeros((head_count, rows, HEAD_DIM), jnp.float32),
    )


def finish_rows(state):
    run_peak, denom, accumulated = state
    heads_out = accumulated / denom[:, :, None]
    rows = heads_out.shape[1]
    return (
        heads_out.transpose(1, 0, 2)
        .reshape(rows, heads_out.shape[0] * heads_out.shape[2])
        .astype(jnp.bfloat16)
    )


def per_device(resid_in, feats, short_filter, residues, rates, out_weight, norm_gain, attn_weight):
    row_count, chan_count = resid_in.shape
    width_all = out_weight.shape[1]
    short_out = short_mix(feats, short_filter)
    product = (short_out[:, 1] * short_out[:, 2]).astype(jnp.bfloat16)
    panel_rows = lax.all_to_all(product.T, "ctx", split_axis=0, concat_axis=1, tiled=True)
    panel_count = chan_count // lax.axis_size("ctx")
    panel_start = lax.axis_index("ctx") * panel_count
    panel_res = lax.dynamic_slice_in_dim(residues, panel_start, panel_count, 0)
    panel_rates = lax.dynamic_slice_in_dim(rates, panel_start, panel_count, 0)
    panel_conv = modal_conv(
        panel_rows.astype(jnp.float32), panel_res, panel_rates, jnp.zeros_like(panel_rates)
    )
    returned = lax.all_to_all(panel_conv, "ctx", split_axis=1, concat_axis=0, tiled=True)
    conv_out = returned.T
    gated = (short_out[:, 0] * conv_out).astype(jnp.bfloat16)
    own_share = lax.psum_scatter(
        lax.dot_general(
            out_weight, gated, (((0,), (1,)), ((), ())), preferred_element_type=jnp.float32
        ),
        "tp",
        scatter_dimension=0,
        tiled=True,
    )
    hyena_out = (resid_in.astype(jnp.float32) + own_share.T).astype(jnp.bfloat16)
    full_rows = lax.all_gather(hyena_out, "tp", axis=1, tiled=True)
    wide = full_rows.astype(jnp.float32)
    mean_square = jnp.mean(wide * wide, axis=1, keepdims=True)
    normed = (wide * lax.rsqrt(mean_square + eps_norm) * norm_gain).astype(jnp.bfloat16)
    projected = jnp.dot(
        normed, attn_weight.reshape(width_all, 3 * chan_count), preferred_element_type=jnp.float32
    ).reshape(row_count, 3, chan_count)
    head_count = chan_count // HEAD_DIM
    ctx_index = lax.axis_index("ctx")
    first_pos = ctx_index * row_count
    positions = first_pos + jnp.arange(row_count, dtype=jnp.int32)
    queries = rotary_turn(
        projected[:, 0].reshape(row_count, head_count, HEAD_DIM), positions
    ).astype(jnp.bfloat16)
    keys_all = rotary_turn(
        projected[:, 1].reshape(row_count, head_count, HEAD_DIM), positions
    ).astype(jnp.bfloat16)
    values = projected[:, 2].astype(jnp.bfloat16)
    key_pieces = (keys_all.reshape(row_count, chan_count), values)
    initial = empty_state(head_count, row_count)
    key_rows = lax.all_gather(key_pieces[0], "ctx", axis=0, tiled=True)
    value_rows = lax.all_gather(key_pieces[1], "ctx", axis=0, tiled=True)
    key_total = key_rows.shape[0]
    tiles_block_size = math.gcd(key_total, 1024)
    block_count = key_total // tiles_block_size
    key_blocks = key_rows.reshape(block_count, tiles_block_size, head_count, HEAD_DIM)
    value_blocks = value_rows.reshape(block_count, tiles_block_size, head_count, HEAD_DIM)
    key_blocks, value_blocks, block_ids, block_size = (
        key_blocks,
        value_blocks,
        jnp.arange(block_count, dtype=jnp.int32),
        tiles_block_size,
    )

    def one_tile(carried, slot_item):
        key_block, value_block, block_index = slot_item
        key_start = block_index * block_size
        updated = attend_tile(carried, queries, positions, key_block, value_block, key_start)
        return (updated, None)

    result, _ = lax.scan(one_tile, initial, (key_blocks, value_blocks, block_ids))
    context = finish_rows(result)
    return (hyena_out, context)


def solution(mesh):
    in_specs = (
        P("ctx", "tp"),
        P("ctx", None, "tp"),
        P(None, None, "tp"),
        P("tp", None),
        P("tp", None),
        P("tp", None),
        P(),
        P(None, None, "tp"),
    )
    out_specs = (P("ctx", "tp"), P("ctx", "tp"))
    return jax.shard_map(
        per_device, mesh=mesh, in_specs=in_specs, out_specs=out_specs, check_vma=False
    )
```

profile of v0, /device:TPU:4, one launch (start us, length us, event | category | flops | bytes accessed | tf_op | source)
XLA Modules:
  0.0 341.5 jit_solution(16704651836069771264)
XLA Ops:
  7.2 0.8 slice.59
  8.1 3.4 %collective-permute-start = (bf16[2,3,128]{0,2,1:T(8,128)(2,1)S(1)}, bf16[2,3,128]{0,2,1:T(8,128)(2,1)S(1)}, u32[]{:S(2)}, u32[]{:S(2)}) collective-permute-start(bf16[2,3,128]{0,2,1:T(8,128)(2,1)S(1)} %copy.44), channel_id=1, source_target_pairs={{0,32},{32,64},{64,96},{96,128},{128,160},{160,192},{192,224},{224... | collective-permute-start | bytes 4616 | tf_op jit(solution)/shard_map/ppermute | solution.py:17
  11.8 0.8 constant_dynamic-slice_fusion
  12.7 0.7 slice_bitcast_fusion.3
  13.5 1.0 copy.45
  14.9 0.6 tile.10
  15.9 1.6 reshape.257
  18.4 0.6 fusion.65
  19.0 8.8 %all-to-all-start = ((bf16[16,8,128]{2,1,0:T(8,128)(2,1)}), bf16[16,8,128]{2,1,0:T(8,128)(2,1)S(1)}, u32[]{:S(2)}, u32[]{:S(2)}) async-start(bf16[16,8,128]{2,1,0:T(8,128)(2,1)} %fusion.65), calls=%async_computation | async-start | bytes 65536 | tf_op jit(solution)/shard_map/all_to_all | solution.py:134
  27.8 7.4 %all-to-all-done = bf16[16,8,128]{2,1,0:T(8,128)(2,1)S(1)} async-done(((bf16[16,8,128]{2,1,0:T(8,128)(2,1)}), bf16[16,8,128]{2,1,0:T(8,128)(2,1)S(1)}, u32[]{:S(2)}, u32[]{:S(2)}) %all-to-all-start) | async-done | bytes 32800 | tf_op jit(solution)/shard_map/all_to_all | solution.py:134
  37.0 13.1 %all_to_all.32 = f32[8,16,128]{2,0,1:T(8,128)S(1)} all-to-all(f32[8,16,128]{2,0,1:T(8,128)S(1)} %copy.49), channel_id=1, replica_groups=mesh['ctx'=16,'tp'=32] {'ctx'}, dimensions={1} | all-to-all | bytes 131072 | tf_op jit(solution)/shard_map/all_to_all | solution.py:142
  50.2 1.8 convolution_bitcast_fusion.1
  52.1 122.4 %reduce-scatter.2.cloned.1.call-done = f32[128,128]{0,1:T(8,128)} async-done(((f32[4096,128]{0,1:T(8,128)}), f32[128,128]{0,1:T(8,128)}) %reduce-scatter.2.cloned.1.call-update) | async-done | bytes 65552 | tf_op jit(solution)/shard_map/reduce_scatter | solution.py:145
  174.4 1.5 fusion.39
  176.0 4.7 %copy.50 = bf16[4096,3,128]{0,2,1:T(8,128)(2,1)} copy(bf16[4096,3,128]{2,0,1:T(8,128)(2,1)} %param.17) | data formatting | bytes 6291456 | tf_op args[7]
  180.7 59.4 %all-gather.3.cloned.1.call-done = bf16[128,4096]{1,0:T(8,128)(2,1)} async-done(((bf16[128,128]{1,0:T(8,128)(2,1)}), bf16[128,4096]{1,0:T(8,128)(2,1)}) %all-gather.3.cloned.1.call-update) | async-done | bytes 1048592 | tf_op jit(solution)/shard_map/all_gather | solution.py:154
  240.1 1.5 fusion.25
  241.6 3.3 fusion.23
  245.3 39.5 %all_gather.10 = bf16[2048,128]{0,1:T(8,128)(2,1)S(1)} all-gather(bf16[128,128]{0,1:T(8,128)(2,1)S(1)} %pad_maximum_fusion), channel_id=1, replica_groups=mesh['ctx'=16,'tp'=32] {'ctx'}, dimensions={0}, use_global_device_ids=true | all-gather | bytes 557056 | tf_op jit(solution)/shard_map/all_gather | solution.py:174
  285.0 44.0 %all-gather = bf16[2048,1,128]{0,2,1:T(8,128)(2,1)S(1)} all-gather(bf16[128,1,128]{0,2,1:T(8,128)(2,1)S(1)} %slice.136), channel_id=2, replica_groups=mesh['ctx'=16,'tp'=32] {'ctx'}, dimensions={0}, use_global_device_ids=true | all-gather | bytes 557056 | tf_op jit(solution)/shard_map/all_gather | solution.py:175
  329.3 4.6 %while.15 = (s32[]{:T(128)}, f32[1,128]{1,0:T(1,128)S(1)}, f32[1,128]{1,0:T(1,128)S(1)}, f32[1,128,128]{2,1,0:T(8,128)S(1)}, s32[2]{0:T(128)S(1)}, /*index=5*/bf...) while((s32[]{:T(128)}, f32[1,128]{1,0:T(1,128)S(1)}, ...), condition=%wide.region_6.7_spmd.clone, body=%wide.region_3.6_spmd.clone.sunk | while | flops 68732800 | bytes 2287785 | solution.py:194
  329.3 0.6 dynamic_slice.39
  331.6 0.6 dynamic_slice.39
  333.9 0.7 fusion.74
  (64 shorter events, 7.0 us)
Async XLA Ops:
  7.2 43.0 %copy-start = (bf16[128,4096]{1,0:T(8,128)(2,1)S(1)}, bf16[128,4096]{1,0:T(8,128)(2,1)}, u32[]{:S(2)}) copy-start(bf16[128,4096]{1,0:T(8,128)(2,1)} %param.15) | copy-start | bytes 3145732
  8.1 9.7 %collective-permute-start = (bf16[2,3,128]{0,2,1:T(8,128)(2,1)S(1)}, bf16[2,3,128]{0,2,1:T(8,128)(2,1)S(1)}, u32[]{:S(2)}, u32[]{:S(2)}) collective-permute-start(bf16[2,3,128]{0,2,1:T(8,128)(2,1)S(1)} %copy.44), channel_id=1, source_target_pairs={{0,32},{32,64},{64,96},{96,128},{128,160},{160,192},{192,224},{224... | collective-permute-start | bytes 4616 | tf_op jit(solution)/shard_map/ppermute | solution.py:17
  19.0 16.2 %all-to-all-start = ((bf16[16,8,128]{2,1,0:T(8,128)(2,1)}), bf16[16,8,128]{2,1,0:T(8,128)(2,1)S(1)}, u32[]{:S(2)}, u32[]{:S(2)}) async-start(bf16[16,8,128]{2,1,0:T(8,128)(2,1)} %fusion.65), calls=%async_computation | async-start | bytes 65536 | tf_op jit(solution)/shard_map/all_to_all | solution.py:134
  27.8 146.7 %reduce-scatter.2.cloned.1.call-start = ((), (), s32[]{:S(2)}) async-start(), calls=%async_computation.3 | async-start | bytes 2162688 | tf_op jit(solution)/shard_map/reduce_scatter | solution.py:145
  50.2 124.3 %copy-start.1 = (bf16[128,128]{1,0:T(8,128)(2,1)S(1)}, bf16[128,128]{1,0:T(8,128)(2,1)}, u32[]{:S(2)}) copy-start(bf16[128,128]{1,0:T(8,128)(2,1)} %param.10) | copy-start | bytes 98308
  52.0 188.1 %all-gather.3.cloned.1.call-start = ((), (), s32[]{:S(2)}) async-start(), calls=%async_computation.4 | async-start | bytes 1081344 | tf_op jit(solution)/shard_map/all_gather | solution.py:154
  175.9 65.7 %copy-start.2 = (f32[4096]{0:T(1024)S(1)}, f32[4096]{0:T(1024)}, u32[]{:S(2)}) copy-start(f32[4096]{0:T(1024)} %param.16) | copy-start | bytes 49156
Sparse Core Ops, SparseCore 0:
  52.1 122.2 reduce-scatter.1
  177.3 62.7 all-gather.2
where the time goes:
time: 342 us; the launch traced here: 341 us
  waiting for transfers between devices  190 us (56%)
  blocking collectives  96.6 us (28%)
  between operations  14.3 us (4%)
  local copies, waits for them, and re-layouts  13.3 us (4%)
  starting transfers between devices  12.3 us (4%)
  matrix products  7.62 us (2%)
  other arithmetic  6.38 us (2%)
    reduce_scatter x1, waiting for transfers between devices, per_device(): lax.psum_scatter(lax.dot_general(out_weight, gated, (((0,), (1,)), ((), (...  122 us
    all_gather x1, waiting for transfers between devices, per_device(): full_rows = lax.all_gather(hyena_out, 'tp', axis=1, tiled=True)  59.4 us
    all_gather x1, blocking collectives, per_device(): value_rows = lax.all_gather(key_pieces[1], 'ctx', axis=0, tiled=True)  44 us
    all_gather x1, blocking collectives, per_device(): key_rows = lax.all_gather(key_pieces[0], 'ctx', axis=0, tiled=True)  39.5 us
    all_to_all x1, blocking collectives, per_device(): lax.all_to_all(panel_conv, 'ctx', split_axis=1, concat_axis=0, tiled=True)  13.1 us
    all_to_all x1, starting transfers between devices, per_device(): lax.all_to_all(product.T, 'ctx', split_axis=0, concat_axis=1, tiled=True)  8.78 us
    all_to_all x1, waiting for transfers between devices, per_device(): lax.all_to_all(product.T, 'ctx', split_axis=0, concat_axis=1, tiled=True)  7.39 us
  transfers between devices with their start and end apart: 4, of which 4 were waited for; matrix products, arithmetic and copies ran while one was open for 3% of the time, Pallas kernels for 0%

commit v1 on v0

--- a/solution.py
+++ b/solution.py
@@ -131,7 +131,10 @@
     width_all = out_weight.shape[1]
     short_out = short_mix(feats, short_filter)
     product = (short_out[:, 1] * short_out[:, 2]).astype(jnp.bfloat16)
-    panel_rows = lax.all_to_all(product.T, "ctx", split_axis=0, concat_axis=1, tiled=True)
+    panel_rows = jnp.concatenate(
+        lax.all_to_all(jnp.stack(jnp.split(product.T, lax.axis_size("ctx"), axis=0)), "ctx", 0, 0),
+        axis=1,
+    )
     panel_count = chan_count // lax.axis_size("ctx")
     panel_start = lax.axis_index("ctx") * panel_count
     panel_res = lax.dynamic_slice_in_dim(residues, panel_start, panel_count, 0)

time: 342 us -> 351 us (1.026)
  local copies, waits for them, and re-layouts: 13.3 us -> 22.6 us
    unnamed x16 -> x31, local copies, waits for them, and re-layouts: 6.83 us -> 15.5 us
where the time goes in v1:
time: 351 us
  waiting for transfers between devices  190 us (54%)
  blocking collectives  96.6 us (28%)
  local copies, waits for them, and re-layouts  22.6 us (6%)
  between operations  14.3 us (4%)
  starting transfers between devices  12.3 us (4%)
  matrix products  7.62 us (2%)
  other arithmetic  5.78 us (2%)
    reduce_scatter x1, waiting for transfers between devices, per_device(): lax.psum_scatter(lax.dot_general(out_weight, gated, (((0,), (1,)), ((), (...  122 us
    all_gather x1, waiting for transfers between devices, per_device(): full_rows = lax.all_gather(hyena_out, 'tp', axis=1, tiled=True)  59.8 us
    all_gather x1, blocking collectives, per_device(): value_rows = lax.all_gather(key_pieces[1], 'ctx', axis=0, tiled=True)  44 us
    all_gather x1, blocking collectives, per_device(): key_rows = lax.all_gather(key_pieces[0], 'ctx', axis=0, tiled=True)  39.5 us
    unnamed x31, local copies, waits for them, and re-layouts  15.5 us
    all_to_all x1, blocking collectives, per_device(): lax.all_to_all(panel_conv, 'ctx', split_axis=1, concat_axis=0, tiled=True)  13.1 us
    all_to_all x1, starting transfers between devices, per_device(): lax.all_to_all(jnp.stack(jnp.split(product.T, lax.axis_size('ctx'), axis=...  8.79 us
    all_to_all x1, waiting for transfers between devices, per_device(): lax.all_to_all(jnp.stack(jnp.split(product.T, lax.axis_size('ctx'), axis=...  7.39 us
  transfers between devices with their start and end apart: 4, of which 4 were waited for; matrix products, arithmetic and copies ran while one was open for 3% of the time, Pallas kernels for 0%

profile of v1, /device:TPU:4, one launch (start us, length us, event | category | flops | bytes accessed | tf_op | source)
XLA Modules:
  0.0 350.5 jit_solution(13204490716095338247)
XLA Ops:
  7.2 0.8 slice.59
  8.1 3.4 collective-permute-start
  11.8 0.7 slice_bitcast_fusion.19
  12.5 0.8 constant_dynamic-slice_fusion
  13.5 1.0 copy.510
  14.9 0.6 tile.10
  15.9 1.6 reshape.259
  18.4 0.6 constant_dynamic-update-slice_fusion.15
  27.6 8.8 %all-to-all-start = ((bf16[16,8,128]{2,1,0:T(8,128)(2,1)}), bf16[16,8,128]{2,1,0:T(8,128)(2,1)S(1)}, u32[]{:S(2)}, u32[]{:S(2)}) async-start(bf16[16,8,128]{2,1,0:T(8,128)(2,1)} %constant_dynamic-update-slice_fusion), calls=%async_computation | async-start | bytes 65536 | tf_op jit(solution)/shard_map/all_to_all | solution.py:135
  36.5 7.4 %all-to-all-done = bf16[16,8,128]{2,1,0:T(8,128)(2,1)S(1)} async-done(((bf16[16,8,128]{2,1,0:T(8,128)(2,1)}), bf16[16,8,128]{2,1,0:T(8,128)(2,1)S(1)}, u32[]{:S(2)}, u32[]{:S(2)}) %all-to-all-start) | async-done | bytes 32800 | tf_op jit(solution)/shard_map/all_to_all | solution.py:135
  45.7 13.1 %all_to_all.21 = f32[8,16,128]{2,0,1:T(8,128)S(1)} all-to-all(f32[8,16,128]{2,0,1:T(8,128)S(1)} %copy.514), channel_id=1, replica_groups=mesh['ctx'=16,'tp'=32] {'ctx'}, dimensions={1} | all-to-all | bytes 131072 | tf_op jit(solution)/shard_map/all_to_all | solution.py:145
  58.8 1.8 convolution_bitcast_fusion.1
  60.7 122.3 %reduce-scatter.2.cloned.1.call-done = f32[128,128]{0,1:T(8,128)} async-done(((f32[4096,128]{0,1:T(8,128)}), f32[128,128]{0,1:T(8,128)}) %reduce-scatter.2.cloned.1.call-update) | async-done | bytes 65552 | tf_op jit(solution)/shard_map/reduce_scatter | solution.py:148
  183.1 1.5 fusion.39
  184.6 4.7 %copy.515 = bf16[4096,3,128]{0,2,1:T(8,128)(2,1)} copy(bf16[4096,3,128]{2,0,1:T(8,128)(2,1)} %param.17) | data formatting | bytes 6291456 | tf_op args[7]
  189.3 59.8 %all-gather.3.cloned.1.call-done = bf16[128,4096]{1,0:T(8,128)(2,1)} async-done(((bf16[128,128]{1,0:T(8,128)(2,1)}), bf16[128,4096]{1,0:T(8,128)(2,1)}) %all-gather.3.cloned.1.call-update) | async-done | bytes 1048592 | tf_op jit(solution)/shard_map/all_gather | solution.py:157
  249.1 1.5 fusion.25
  250.6 3.3 fusion.23
  254.3 39.5 %all_gather.10 = bf16[2048,128]{0,1:T(8,128)(2,1)S(1)} all-gather(bf16[128,128]{0,1:T(8,128)(2,1)S(1)} %pad_maximum_fusion), channel_id=1, replica_groups=mesh['ctx'=16,'tp'=32] {'ctx'}, dimensions={0}, use_global_device_ids=true | all-gather | bytes 557056 | tf_op jit(solution)/shard_map/all_gather | solution.py:177
  294.0 44.0 %all-gather = bf16[2048,1,128]{0,2,1:T(8,128)(2,1)S(1)} all-gather(bf16[128,1,128]{0,2,1:T(8,128)(2,1)S(1)} %slice.136), channel_id=2, replica_groups=mesh['ctx'=16,'tp'=32] {'ctx'}, dimensions={0}, use_global_device_ids=true | all-gather | bytes 557056 | tf_op jit(solution)/shard_map/all_gather | solution.py:178
  338.3 4.6 %while.15 = (s32[]{:T(128)}, f32[1,128]{1,0:T(1,128)S(1)}, f32[1,128]{1,0:T(1,128)S(1)}, f32[1,128,128]{2,1,0:T(8,128)S(1)}, s32[2]{0:T(128)S(1)}, /*index=5*/bf...) while((s32[]{:T(128)}, f32[1,128]{1,0:T(1,128)S(1)}, ...), condition=%wide.region_6.7_spmd.clone, body=%wide.region_3.6_spmd.clone.sunk | while | flops 68732800 | bytes 2287785 | solution.py:197
  338.3 0.6 dynamic_slice.39
  340.7 0.6 dynamic_slice.39
  343.0 0.7 fusion.74
  (80 shorter events, 15.7 us)
Async XLA Ops:
  7.2 51.7 %copy-start = (bf16[128,4096]{1,0:T(8,128)(2,1)S(1)}, bf16[128,4096]{1,0:T(8,128)(2,1)}, u32[]{:S(2)}) copy-start(bf16[128,4096]{1,0:T(8,128)(2,1)} %param.15) | copy-start | bytes 3145732
  8.1 9.7 %collective-permute-start = (bf16[2,3,128]{0,2,1:T(8,128)(2,1)S(1)}, bf16[2,3,128]{0,2,1:T(8,128)(2,1)S(1)}, u32[]{:S(2)}, u32[]{:S(2)}) collective-permute-start(bf16[2,3,128]{0,2,1:T(8,128)(2,1)S(1)} %copy.509), channel_id=1, source_target_pairs={{0,32},{32,64},{64,96},{96,128},{128,160},{160,192},{192,224},{224... | collective-permute-start | bytes 4616 | tf_op jit(solution)/shard_map/ppermute | solution.py:17
  27.6 16.2 %all-to-all-start = ((bf16[16,8,128]{2,1,0:T(8,128)(2,1)}), bf16[16,8,128]{2,1,0:T(8,128)(2,1)S(1)}, u32[]{:S(2)}, u32[]{:S(2)}) async-start(bf16[16,8,128]{2,1,0:T(8,128)(2,1)} %constant_dynamic-update-slice_fusion), calls=%async_computation | async-start | bytes 65536 | tf_op jit(solution)/shard_map/all_to_all | solution.py:135
  36.4 146.6 %reduce-scatter.2.cloned.1.call-start = ((), (), s32[]{:S(2)}) async-start(), calls=%async_computation.3 | async-start | bytes 2162688 | tf_op jit(solution)/shard_map/reduce_scatter | solution.py:148
  58.8 124.2 %copy-start.1 = (bf16[128,128]{1,0:T(8,128)(2,1)S(1)}, bf16[128,128]{1,0:T(8,128)(2,1)}, u32[]{:S(2)}) copy-start(bf16[128,128]{1,0:T(8,128)(2,1)} %param.10) | copy-start | bytes 98308
  60.7 188.4 %all-gather.3.cloned.1.call-start = ((), (), s32[]{:S(2)}) async-start(), calls=%async_computation.4 | async-start | bytes 1081344 | tf_op jit(solution)/shard_map/all_gather | solution.py:157
  184.6 66.0 %copy-start.2 = (f32[4096]{0:T(1024)S(1)}, f32[4096]{0:T(1024)}, u32[]{:S(2)}) copy-start(f32[4096]{0:T(1024)} %param.16) | copy-start | bytes 49156
Sparse Core Ops, SparseCore 0:
  60.8 122.2 reduce-scatter.1
  185.9 63.1 all-gather.2
